TPU v7x, 32 devices: a whole 2x2x4 slice. The times are simulated.
32 devices in a mesh: grp: 2 (over x), row: 16 (over z, y, core).
Axes of the slice: x: 2, y: 2, z: 4, core: 2. Of those that a mesh axis runs over, the one named last changes fastest.
Arguments:
- panels: bfloat16 [3, 8192, 1536], P(None, 'row'), may hold values from -0.099436891 to 0.099436891, as said below
- first_f: bfloat16 [1536, 512], P('row', 'grp'), parts along dimension 1, may hold values from -6 to 6
- first_g: bfloat16 [1536, 512], P('row', 'grp'), parts along dimension 1, may hold values from -6 to 6
- phase: float32 [4, 1536], P('grp'), parts along dimension 0, may hold values from -3.140625 to 3.140625
- wavenum: float32 [4, 1536], P('grp'), parts along dimension 0, may hold values from 0.5 to 2
Outputs:
- final_f: float32 [1536, 512], P('row', 'grp'), parts along dimension 1
- final_g: float32 [1536, 512], P('row', 'grp'), parts along dimension 1
There are 2 independent parts, one for each index of `grp`. A program takes and returns all parts, laid end to end along the dimension named above; an argument that names none is the same for every part. Nothing has to cross between parts.
Inputs may be any that keep to these rules, and one draw needn't show every extreme that they name: `panels`: consecutive sectors' surface functions share part of their shape.
All inputs are finite; a program needn't handle non-finite values.
Results may differ from a plain program's by a relative error of at most 0.013.
Values may be sent and summed in bfloat16 or wider, within the bound.
No kernel may reach another device: no remote copies, remote signals or barrier semaphores. Data moves between devices by JAX's collectives and lax.ppermute only.
A program may use at most 64 MiB of HBM per device.

v0:
```python
import jax
import jax.numpy as jnp
from jax import lax
from jax.sharding import PartitionSpec as P

SECTORS = 2


def contract_rows(left, right):
    return lax.dot_general(
        left, right, (((0,), (0,)), ((), ())), preferred_element_type=jnp.float32
    )


def shards(panels, first_f, first_g, phase, wavenum):
    chan_rows = first_f.shape[0]
    width = first_f.shape[1]
    all_channels = chan_rows * lax.axis_size("row")
    first_row = lax.axis_index("row") * chan_rows
    solutions = lax.all_gather(
        jnp.concatenate([first_f, first_g], axis=1), "row", axis=0, tiled=True
    )
    for sector in range(SECTORS):
        projected = jnp.dot(panels[sector], solutions, preferred_element_type=jnp.float32).astype(
            jnp.bfloat16
        )
        rotated = lax.psum(contract_rows(panels[sector + 1], projected), "row")
        rot_amp = rotated[:, :width]
        rot_der = rotated[:, width:]
        cosine = jnp.cos(phase[sector])[:, None]
        sine = jnp.sin(phase[sector])[:, None]
        wave = wavenum[sector][:, None]
        new_amp = cosine * rot_amp + sine / wave * rot_der
        new_der = -wave * sine * rot_amp + cosine * rot_der
        norm = jnp.sum(new_amp * new_amp, axis=0) + jnp.sum(new_der * new_der, axis=0)
        scale = 1.0 / jnp.sqrt(norm / (2.0 * all_channels) + 1e-06)
        amp = new_amp * scale[None, :]
        der = new_der * scale[None, :]
        solutions = jnp.concatenate([amp, der], axis=1).astype(jnp.bfloat16)
    amp = lax.dynamic_slice_in_dim(amp, first_row, chan_rows, 0)
    der = lax.dynamic_slice_in_dim(der, first_row, chan_rows, 0)
    return (amp, der)


def solution(mesh):
    in_specs = (
        P(None, "row", None),
        P("row", "grp"),
        P("row", "grp"),
        P("grp", None),
        P("grp", None),
    )
    out_specs = (P("row", "grp"), P("row", "grp"))
    return jax.shard_map(shards, mesh=mesh, in_specs=in_specs, out_specs=out_specs, check_vma=False)
```

profile of v0, /device:TPU:0, one launch (start us, length us, event | category | flops | bytes accessed | tf_op | source)
XLA Modules:
  0.0 283.9 jit_solution(17807892676333385672)
XLA Ops:
  7.2 0.0 all-gather.2.cloned.1.call-start
  7.2 1.5 pad_maximum_fusion
  8.7 0.0 all-gather.2.cloned.1.call-update
  8.7 0.0 all-reduce.3.cloned.1.call-start
  8.8 44.5 %all-gather.2.cloned.1.call-done = bf16[1536,512]{1,0:T(8,128)(2,1)} async-done(((bf16[96,512]{1,0:T(8,128)(2,1)}), bf16[1536,512]{1,0:T(8,128)(2,1)}) %all-gather.2.cloned.1.call-update) | async-done | bytes 1572880 | tf_op jit(solution)/shard_map/all_gather | solution.py:20
  53.3 5.9 %convolution_bitcast_fusion.1 = f32[1536,512]{0,1:T(8,128)} fusion(bf16[3,512,1536]{2,1,0:T(8,128)(2,1)} %param.5, bf16[1536,512]{1,0:T(8,128)(2,1)} %all-gather.2.cloned.1.call-done), kind=kOutput, calls=%fused_computation.1 | convolution fusion | flops 1610874880 | bytes 7864320 | tf_op jit(solution)/shard_map/dot_general | solution.py:10
  59.1 0.0 copy-start.1
  59.1 0.0 copy-start.2
  59.1 0.0 all-reduce.3.cloned.1.call-update
  59.2 0.0 all-reduce.5.cloned.1.call-start
  59.2 0.6 copy-done.1
  59.9 0.0 copy-done.2
  59.9 0.4 cosine_reduce_fusion.1
  60.3 101.2 %all-reduce.3.cloned.1.call-done = f32[1536,512]{0,1:T(8,128)} async-done(((f32[1536,512]{0,1:T(8,128)}), f32[1536,512]{0,1:T(8,128)}) %all-reduce.3.cloned.1.call-update) | async-done | bytes 3145744 | tf_op jit(solution)/shard_map/psum | solution.py:27
  161.5 0.0 copy-start
  161.5 2.7 multiply_reduce_fusion.2
  164.2 0.2 copy-done
  164.3 0.5 multiply_convert_fusion.1
  164.9 5.4 %convolution_bitcast_fusion = f32[1536,512]{0,1:T(8,128)} fusion(bf16[3,512,1536]{2,1,0:T(8,128)(2,1)} %param.5, bf16[1536,256]{0,1:T(8,128)(2,1)S(1)} %get-tuple-element.17, bf16[1536,256]{0,1:T(8,128)(2,1)S(1)} %get-tuple-element.16), kind=kOutput, calls=%fused_computation | convolution fusion | flops 1614020608 | bytes 7864320 | tf_op jit(solution)/shard_map/dot_general | solution.py:10
  170.3 0.0 all-reduce.5.cloned.1.call-update
  170.3 102.9 %all-reduce.5.cloned.1.call-done = f32[1536,512]{0,1:T(8,128)} async-done(((f32[1536,512]{0,1:T(8,128)}), f32[1536,512]{0,1:T(8,128)}) %all-reduce.5.cloned.1.call-update) | async-done | bytes 3145744 | tf_op jit(solution)/shard_map/psum | solution.py:27
  273.2 2.5 multiply_reduce_fusion
  275.7 0.2 dynamic-slice_multiply_fusion
  275.9 0.7 copy.7
  276.6 0.7 copy.8
  (5 shorter events, 0.1 us)
Async XLA Ops:
  7.2 46.1 %all-gather.2.cloned.1.call-start = ((), (), s32[]{:S(2)}) async-start(), calls=%async_computation | async-start | bytes 1671168 | tf_op jit(solution)/shard_map/all_gather | solution.py:20
  8.7 152.8 %all-reduce.3.cloned.1.call-start = ((), (), s32[]{:S(2)}) async-start(), calls=%async_computation.1 | async-start | bytes 6291456 | tf_op jit(solution)/shard_map/psum | solution.py:27
  59.1 0.7 copy-start.1
  59.1 0.7 copy-start.2
  59.2 214.0 %all-reduce.5.cloned.1.call-start = ((), (), s32[]{:S(2)}) async-start(), calls=%async_computation.2 | async-start | bytes 6291456 | tf_op jit(solution)/shard_map/psum | solution.py:27
  161.5 2.8 copy-start
Sparse Core Ops, SparseCore 0:
  10.9 42.3 all-gather.1
  59.3 102.1 all-reduce.2
  170.4 102.7 all-reduce.4
where the time goes:
time: 284 us
  waiting for transfers between devices  249 us (88%)
  between operations  13.8 us (5%)
  matrix products  11.3 us (4%)
  other arithmetic  7.44 us (3%)
    psum x2, waiting for transfers between devices, shards(): rotated = lax.psum(contract_rows(panels[sector + 1], projected), 'row')  204 us
    all_gather x1, waiting for transfers between devices, shards(): lax.all_gather(jnp.concatenate([first_f, first_g], axis=1), 'row', axis=0...  44.5 us
    dot_general x2, matrix products, contract_rows(): lax.dot_general(left, right, (((0,), (0,)), ((), ())), preferred_element_...  11.3 us
  transfers between devices with their start and end apart: 3, of which 3 were waited for; matrix products, arithmetic and copies ran while one was open for 0% of the time, Pallas kernels for 0%

commit v1 on v0

--- a/solution.py
+++ b/solution.py
@@ -4,6 +4,18 @@
 from jax.sharding import PartitionSpec as P
 
 SECTORS = 2
+
+
+def collect(x, axis, dim):
+    ways, here = (lax.axis_size(axis), lax.axis_index(axis))
+    grown, reach = (x, 1)
+    while reach < ways:
+        theirs = lax.ppermute(grown, axis, [(d, d ^ reach) for d in range(ways)])
+        mine_first = jnp.concatenate([grown, theirs], axis=dim)
+        theirs_first = jnp.concatenate([theirs, grown], axis=dim)
+        grown = jnp.where(here & reach == 0, mine_first, theirs_first)
+        reach = 2 * reach
+    return grown
 
 
 def contract_rows(left, right):
@@ -17,9 +29,7 @@
     width = first_f.shape[1]
     all_channels = chan_rows * lax.axis_size("row")
     first_row = lax.axis_index("row") * chan_rows
-    solutions = lax.all_gather(
-        jnp.concatenate([first_f, first_g], axis=1), "row", axis=0, tiled=True
-    )
+    solutions = collect(jnp.concatenate([first_f, first_g], axis=1), "row", 0)
     for sector in range(SECTORS):
         projected = jnp.dot(panels[sector], solutions, preferred_element_type=jnp.float32).astype(
             jnp.bfloat16

time: 284 us -> 298 us (1.049)
  starting transfers between devices: 0.12 us -> 7.89 us
  waiting for transfers between devices: 249 us -> 254 us
    ppermute x0 -> x4, waiting for transfers between devices: none -> 48.5 us  [collect(): theirs = lax.ppermute(grown, axis, [(d, d ^ reach) for d in range(ways)])]
    all_gather x1 -> x0, waiting for transfers between devices: 44.5 us -> none  [shards(): lax.all_gather(jnp.concatenate([first_f, first_g], axis=1), 'row', axis=0...]
    ppermute x0 -> x4, starting transfers between devices: none -> 7.81 us  [collect(): theirs = lax.ppermute(grown, axis, [(d, d ^ reach) for d in range(ways)])]
  transfers between devices with their start and end apart: 3 -> 6, of which waited for: 3 -> 6; matrix products, arithmetic and copies ran while one was open for 0% -> 0% of each run, Pallas kernels for 0% -> 0%
where the time goes in v1:
time: 298 us
  waiting for transfers between devices  254 us (85%)
  between operations  14.1 us (5%)
  matrix products  10.8 us (4%)
  starting transfers between devices  7.89 us (3%)
  other arithmetic  6.44 us (2%)
  local copies, waits for them, and re-layouts  4.29 us (1%)
    psum x2, waiting for transfers between devices, shards(): rotated = lax.psum(contract_rows(panels[sector + 1], projected), 'row')  206 us
    ppermute x4, waiting for transfers between devices, collect(): theirs = lax.ppermute(grown, axis, [(d, d ^ reach) for d in range(ways)])  48.5 us
    dot_general x2, matrix products, contract_rows(): lax.dot_general(left, right, (((0,), (0,)), ((), ())), preferred_element_...  10.8 us
    ppermute x4, starting transfers between devices, collect(): theirs = lax.ppermute(grown, axis, [(d, d ^ reach) for d in range(ways)])  7.81 us
  transfers between devices with their start and end apart: 6, of which 6 were waited for; matrix products, arithmetic and copies ran while one was open for 0% of the time, Pallas kernels for 0%

profile of v1, /device:TPU:0, one launch (start us, length us, event | category | flops | bytes accessed | tf_op | source)
XLA Modules:
  0.0 297.9 jit_solution(16058147836180715863)
XLA Ops:
  7.2 0.0 all-reduce.3.cloned.1.call-start
  7.2 0.8 constant_dynamic-update-slice_fusion.1
  8.0 0.8 constant_dynamic-update-slice_fusion
  8.8 0.5 collective-permute-start
  9.3 0.9 collective-permute-done
  10.3 2.9 collective-permute-start.1
  13.2 5.2 %collective-permute-done.1 = bf16[192,512]{1,0:T(8,128)(2,1)S(1)} collective-permute-done((bf16[192,512]{1,0:T(8,128)(2,1)S(1)}, bf16[192,512]{1,0:T(8,128)(2,1)S(1)}, u32[]{:S(2)}, u32[]{:S(2)}) %collective-permute-start.1) | collective-permute-done | bytes 196640 | tf_op jit(solution)/shard_map/ppermute | solution.py:13
  18.4 0.1 maximum_select_fusion.7
  18.5 1.9 collective-permute-start.2
  20.4 8.9 %collective-permute-done.2 = bf16[384,512]{1,0:T(8,128)(2,1)S(1)} collective-permute-done((bf16[384,512]{1,0:T(8,128)(2,1)S(1)}, bf16[384,512]{1,0:T(8,128)(2,1)S(1)}, u32[]{:S(2)}, u32[]{:S(2)}) %collective-permute-start.2) | collective-permute-done | bytes 393248 | tf_op jit(solution)/shard_map/ppermute | solution.py:13
  29.3 0.3 maximum_select_fusion.6
  29.6 2.6 collective-permute-start.3
  32.1 33.5 %collective-permute-done.3 = bf16[768,512]{1,0:T(8,128)(2,1)S(1)} collective-permute-done((bf16[768,512]{1,0:T(8,128)(2,1)S(1)}, bf16[768,512]{1,0:T(8,128)(2,1)S(1)}, u32[]{:S(2)}, u32[]{:S(2)}) %collective-permute-start.3) | collective-permute-done | bytes 786464 | tf_op jit(solution)/shard_map/ppermute | solution.py:13
  65.6 5.4 %convolution_bitcast_fusion.1 = f32[1536,512]{0,1:T(8,128)} fusion(bf16[3,512,1536]{2,1,0:T(8,128)(2,1)} %param.5, bf16[768,512]{1,0:T(8,128)(2,1)S(1)} %collective-permute-done.3, bf16[768,512]{1,0:T(8,128)(2,1)S(1)} %maximum_select_fusion.6, pred[]{:T(512)S(6)} %eq.12), kind=kOutput, calls=%fused_computation.1 | convolution fusion | flops 1617952768 | bytes 7864321 | tf_op jit(solution)/shard_map/dot_general | solution.py:22
  71.0 0.0 copy-start.1
  71.0 0.0 copy-start.2
  71.0 0.0 all-reduce.3.cloned.1.call-update
  71.0 0.0 all-reduce.5.cloned.1.call-start
  71.1 0.6 copy-done.1
  71.8 0.0 copy-done.2
  71.8 0.4 cosine_reduce_fusion.1
  72.2 103.1 %all-reduce.3.cloned.1.call-done = f32[1536,512]{0,1:T(8,128)} async-done(((f32[1536,512]{0,1:T(8,128)}), f32[1536,512]{0,1:T(8,128)}) %all-reduce.3.cloned.1.call-update) | async-done | bytes 3145744 | tf_op jit(solution)/shard_map/psum | solution.py:37
  175.3 2.7 multiply_reduce_fusion.2
  178.0 0.2 copy-done
  178.1 0.5 multiply_convert_fusion.1
  178.7 5.4 %convolution_bitcast_fusion = f32[1536,512]{0,1:T(8,128)} fusion(bf16[3,512,1536]{2,1,0:T(8,128)(2,1)} %param.5, bf16[1536,256]{0,1:T(8,128)(2,1)S(1)} %get-tuple-element.17, bf16[1536,256]{0,1:T(8,128)(2,1)S(1)} %get-tuple-element.16), kind=kOutput, calls=%fused_computation | convolution fusion | flops 1614020608 | bytes 7864320 | tf_op jit(solution)/shard_map/dot_general | solution.py:22
  184.1 0.0 all-reduce.5.cloned.1.call-update
  184.1 102.7 %all-reduce.5.cloned.1.call-done = f32[1536,512]{0,1:T(8,128)} async-done(((f32[1536,512]{0,1:T(8,128)}), f32[1536,512]{0,1:T(8,128)}) %all-reduce.5.cloned.1.call-update) | async-done | bytes 3145744 | tf_op jit(solution)/shard_map/psum | solution.py:37
  286.8 2.5 multiply_reduce_fusion
  289.4 0.2 dynamic-slice_multiply_fusion
  289.6 0.7 copy.7
  290.3 0.7 copy.8
  (7 shorter events, 0.1 us)
Async XLA Ops:
  7.2 168.1 %all-reduce.3.cloned.1.call-start = ((), (), s32[]{:S(2)}) async-start(), calls=%async_computation | async-start | bytes 6291456 | tf_op jit(solution)/shard_map/psum | solution.py:37
  8.8 1.4 collective-permute-start
  10.3 8.2 %collective-permute-start.1 = (bf16[192,512]{1,0:T(8,128)(2,1)S(1)}, bf16[192,512]{1,0:T(8,128)(2,1)S(1)}, u32[]{:S(2)}, u32[]{:S(2)}) collective-permute-start(bf16[192,512]{1,0:T(8,128)(2,1)S(1)} %maximum_select_fusion.8), channel_id=1, source_target_pairs={{0,2},{1,3},{2,0},{3,1},{4,6},{5,7},{6,4},{7,5},{8,10},{9,11},{10,... | collective-permute-start | bytes 589832 | tf_op jit(solution)/shard_map/ppermute | solution.py:13
  18.5 10.7 %collective-permute-start.2 = (bf16[384,512]{1,0:T(8,128)(2,1)S(1)}, bf16[384,512]{1,0:T(8,128)(2,1)S(1)}, u32[]{:S(2)}, u32[]{:S(2)}) collective-permute-start(bf16[384,512]{1,0:T(8,128)(2,1)S(1)} %maximum_select_fusion.7), channel_id=1, source_target_pairs={{0,4},{1,5},{2,6},{3,7},{4,0},{5,1},{6,2},{7,3},{8,12},{9,13},{10,... | collective-permute-start | bytes 1179656 | tf_op jit(solution)/shard_map/ppermute | solution.py:13
  29.6 36.0 %collective-permute-start.3 = (bf16[768,512]{1,0:T(8,128)(2,1)S(1)}, bf16[768,512]{1,0:T(8,128)(2,1)S(1)}, u32[]{:S(2)}, u32[]{:S(2)}) collective-permute-start(bf16[768,512]{1,0:T(8,128)(2,1)S(1)} %maximum_select_fusion.6), channel_id=1, source_target_pairs={{0,8},{1,9},{2,10},{3,11},{4,12},{5,13},{6,14},{7,15},{8,0},{9,1},... | collective-permute-start | bytes 2359304 | tf_op jit(solution)/shard_map/ppermute | solution.py:13
  71.0 0.7 copy-start.1
  71.0 0.7 copy-start.2
  71.0 215.8 %all-reduce.5.cloned.1.call-start = ((), (), s32[]{:S(2)}) async-start(), calls=%async_computation.1 | async-start | bytes 6291456 | tf_op jit(solution)/shard_map/psum | solution.py:37
  175.3 2.8 copy-start
Sparse Core Ops, SparseCore 0:
  71.2 104.0 all-reduce.2
  184.2 102.5 all-reduce.4
